TPU v7x, 256 devices: a whole 4x4x8 slice. The times are simulated.
256 devices in a mesh: segment: 2 (over core), ctx: 64 (over x, z, y_hi), tp: 2 (over y_lo).
Axes of the slice: x: 4, y: 4 (y_hi: 2, y_lo: 2; y = y_hi * 2 + y_lo), z: 8, core: 2. Of those that a mesh axis runs over, the one named last changes fastest.
Arguments:
- queries: bfloat16 [8192, 32, 128], P('ctx', 'tp'), may hold values from -14 to 14
- keys: bfloat16 [8192, 8, 128], P('ctx', 'tp'), may hold values from -10 to 10
- values: bfloat16 [8192, 8, 128], P('ctx', 'tp'), may hold values from -6 to 6
- layer_in: bfloat16 [8192, 4096], P('ctx', 'tp'), may hold values from -6 to 6
- w_bc: bfloat16 [1, 4096, 1024], P(None, 'tp'), may hold values from -0.09375 to 0.09375
- w_dt: bfloat16 [1, 4096, 64], P(None, 'tp'), may hold values from -0.09375 to 0.09375
- dt_bias: float32 [1, 64], P(None, 'tp'), may hold values from -1 to 1
- decay_rate: float32 [1, 64], P(None, 'tp'), may hold values from 1.2207031e-05 to 0.06
- skip_gain: float32 [1, 64], P(None, 'tp'), may hold values from 0.5 to 2
- out_gain: float32 [1, 64, 64], P(None, 'tp'), may hold values from 0.5 to 1.5
Outputs:
- section_out: bfloat16 [2, 8192, 4096], P('segment', 'ctx', 'tp')
All inputs are finite; a program needn't handle non-finite values.
Results may differ from a plain program's by a relative error of at most 0.002.
Values may be sent and summed in bfloat16 or wider, within the bound.
No kernel may reach another device: no remote copies, remote signals or barrier semaphores. Data moves between devices by JAX's collectives and lax.ppermute only.
A program may use at most 256 MiB of HBM per device.

v0:
```python
import math
import jax
import jax.numpy as jnp
from jax import lax
from jax.sharding import PartitionSpec as P

GROUPS = 4
STATE = 128
EPSILON = 1e-05


def prefix(part, axis, combine, identity):
    place = lax.axis_index(axis)
    gathered = jax.tree.map(lambda a: lax.all_gather(a, axis), part)
    state = jax.tree.map(lambda a, e: jnp.zeros_like(a) + jnp.asarray(e, a.dtype), part, identity)

    def one(turn, state):
        return combine(
            state, jax.tree.map(lambda a: lax.dynamic_index_in_dim(a, turn, 0, False), gathered)
        )

    return lax.fori_loop(0, place, one, state)


def swapped(value, axis, distance):
    mask = 2**distance
    pairs = [(source, source ^ mask) for source in range(lax.axis_size(axis))]
    return lax.ppermute(value, axis, pairs)


def span_terms(normed, b_rows, c_rows, step_sizes, rate_row, skip_row):
    count_rows, head_count, head_width = normed.shape
    group_count = b_rows.shape[1]
    per_group = head_count // group_count
    state_root = math.sqrt(b_rows.shape[2])
    log_decay = jnp.cumsum(-step_sizes * rate_row[None, :], axis=0)
    lower_mask = jnp.arange(count_rows)[:, None] >= jnp.arange(count_rows)[None, :]
    intersection = (
        jnp.einsum("tgn,sgn->gts", c_rows, b_rows, precision=lax.Precision.HIGHEST) / state_root
    )
    log_gaps = log_decay.T[:, :, None] - log_decay.T[:, None, :]
    decays = jnp.where(lower_mask[None], jnp.exp(jnp.where(lower_mask[None], log_gaps, 0.0)), 0.0)
    mixing = (
        decays.reshape(group_count, per_group, count_rows, count_rows)
        * intersection[:, None]
        * step_sizes.T.reshape(group_count, per_group, 1, count_rows)
    )
    grouped = normed.reshape(count_rows, group_count, per_group, head_width)
    local_part = jnp.einsum(
        "gkts,sgkp->tgkp", mixing, grouped, precision=lax.Precision.HIGHEST
    ).reshape(count_rows, head_count, head_width)
    tail_weight = jnp.exp(log_decay[-1][None, :] - log_decay) * step_sizes
    weighted = (normed * tail_weight[:, :, None]).reshape(
        count_rows, group_count, per_group, head_width
    )
    ending = jnp.einsum(
        "sgkp,sgn->gkpn", weighted, b_rows, precision=lax.Precision.HIGHEST
    ).reshape(head_count, head_width, b_rows.shape[2])
    return (
        log_decay,
        local_part + skip_row[None, :, None] * normed,
        ending,
        jnp.exp(log_decay[-1]),
    )


def span_inflow(log_decay, c_rows, state_in):
    count_rows, group_count, state_n = c_rows.shape
    head_count, head_width = (state_in.shape[0], state_in.shape[1])
    per_group = head_count // group_count
    state_root = math.sqrt(state_n)
    inflow = jnp.einsum(
        "tgn,gkpn->tgkp",
        c_rows,
        state_in.reshape(group_count, per_group, head_width, state_n),
        precision=lax.Precision.HIGHEST,
    )
    return (
        jnp.exp(log_decay)[:, :, None]
        * inflow.reshape(count_rows, head_count, head_width)
        / state_root
    )


def merge_states(earlier, later):
    return (earlier[0] * later[0], later[0][:, None, None] * earlier[1] + later[1])


def body(queries, keys, values, layer_in, w_bc, w_dt, dt_bias, decay_rate, skip_gain, out_gain):
    segment_index = lax.axis_index("segment")
    attention_on = segment_index == 0
    state_on = jnp.logical_not(attention_on)
    row_count, q_heads, head_width = queries.shape
    kv_heads = keys.shape[1]
    group_size = q_heads // kv_heads
    score_scale = 1.0 / math.sqrt(head_width)
    first_row = lax.axis_index("ctx") * row_count
    last_row = first_row + row_count - 1
    query_place = first_row + jnp.arange(row_count, dtype=jnp.int32)
    grouped = queries.reshape(row_count, kv_heads, group_size, head_width).transpose(1, 2, 0, 3)

    def add_block(carried, key_block, value_block, key_start):
        row_top, row_total, row_sum = carried
        scores = (
            jnp.einsum("kgqd,skd->kgqs", grouped, key_block, preferred_element_type=jnp.float32)
            * score_scale
        )
        key_place = key_start + jnp.arange(key_block.shape[0], dtype=jnp.int32)
        allowed = (query_place[:, None] >= key_place[None, :])[None, None]
        masked = jnp.where(allowed, scores, -1e30)
        new_top = jnp.maximum(row_top, jnp.max(masked, axis=3))
        raw_weight = jnp.where(allowed, jnp.exp(masked - new_top[..., None]), 0.0)
        factor = jnp.exp(row_top - new_top)
        new_total = row_total * factor + jnp.sum(raw_weight, axis=3)
        block_sum = jnp.einsum(
            "kgqs,skd->kgqd",
            raw_weight.astype(jnp.bfloat16),
            value_block,
            preferred_element_type=jnp.float32,
        )
        return (new_top, new_total, row_sum * factor[..., None] + block_sum)

    initial = (
        jnp.full((kv_heads, group_size, row_count), -1e30, jnp.float32),
        jnp.zeros((kv_heads, group_size, row_count), jnp.float32),
        jnp.zeros((kv_heads, group_size, row_count, head_width), jnp.float32),
    )
    key_piece = lax.all_gather(keys, "ctx", axis=0, tiled=True)
    value_piece = lax.all_gather(values, "ctx", axis=0, tiled=True)
    key_count = key_piece.shape[0]
    block_size = math.gcd(key_count, 1024)

    def run_all(inner_state):

        def one_step(block_index, loop_state):
            block_start = block_index * block_size
            key_block = lax.dynamic_slice_in_dim(key_piece, block_start, block_size, 0)
            value_block = lax.dynamic_slice_in_dim(value_piece, block_start, block_size, 0)
            return add_block(loop_state, key_block, value_block, block_start)

        return lax.fori_loop(0, key_count // block_size, one_step, inner_state)

    wanted = jnp.logical_and(attention_on, jnp.int32(0) <= last_row)
    row_top, row_total, row_sum = lax.cond(wanted, run_all, lambda kept_state: kept_state, initial)
    safe_total = jnp.where(attention_on, row_total, 1.0)
    mixed_out = row_sum / safe_total[..., None]
    attended = (
        mixed_out.transpose(2, 0, 1, 3)
        .reshape(row_count, q_heads * head_width)
        .astype(jnp.bfloat16)
    )
    current = layer_in
    channel_count = current.shape[1]
    heads_dev = dt_bias.shape[1]
    state_width = channel_count // heads_dev
    groups_dev = GROUPS // lax.axis_size("tp")
    wide_rows = current.astype(jnp.float32)
    part_bc = jnp.dot(current, w_bc[0], preferred_element_type=jnp.float32)
    part_dt = jnp.dot(current, w_dt[0], preferred_element_type=jnp.float32)
    part_sq = jnp.sum(wide_rows * wide_rows, axis=1)
    sum_bc, sum_dt, sum_sq = lax.psum((part_bc, part_dt, part_sq), "tp")
    inv_rms = lax.rsqrt(sum_sq / (channel_count * lax.axis_size("tp")) + EPSILON)
    normed = (wide_rows * inv_rms[:, None]).reshape(row_count, heads_dev, state_width)
    half_cols = GROUPS * STATE
    b_all = sum_bc[:, :half_cols].reshape(row_count, GROUPS, STATE)
    c_all = sum_bc[:, half_cols:].reshape(row_count, GROUPS, STATE)
    group_start = lax.axis_index("tp") * groups_dev
    b_rows = lax.dynamic_slice_in_dim(b_all, group_start, groups_dev, 1) * inv_rms[:, None, None]
    c_rows = lax.dynamic_slice_in_dim(c_all, group_start, groups_dev, 1) * inv_rms[:, None, None]
    own_dt = lax.dynamic_slice_in_dim(sum_dt, lax.axis_index("tp") * heads_dev, heads_dev, 1)
    step_sizes = jax.nn.softplus(own_dt * inv_rms[:, None] + dt_bias[0][None, :])

    def compute_terms(given):
        return span_terms(given[0], given[1], given[2], given[3], decay_rate[0], skip_gain[0])

    def empty_terms(given):
        return (
            jnp.zeros((row_count, heads_dev), jnp.float32),
            jnp.zeros((row_count, heads_dev, state_width), jnp.float32),
            jnp.zeros((heads_dev, state_width, STATE), jnp.float32),
            jnp.zeros((heads_dev,), jnp.float32),
        )

    log_decay, local_part, ending, span_decay = lax.cond(
        state_on, compute_terms, empty_terms, (normed, b_rows, c_rows, step_sizes)
    )
    decay_in, state_in = prefix(
        (span_decay, ending),
        "ctx",
        merge_states,
        (jnp.ones_like(span_decay), jnp.zeros_like(ending)),
    )
    mixed_out = local_part + span_inflow(log_decay, c_rows, state_in)
    power = jnp.mean(mixed_out * mixed_out, axis=2, keepdims=True)
    result = wide_rows.reshape(row_count, heads_dev, state_width) + out_gain[0][
        None
    ] * mixed_out * lax.rsqrt(power + EPSILON)
    current = result.reshape(row_count, channel_count).astype(jnp.bfloat16)
    result = jnp.where(attention_on, attended, current)
    incoming = swapped(result, "segment", 0)
    return incoming[None]


def solution(mesh):
    in_specs = (
        P("ctx", "tp", None),
        P("ctx", "tp", None),
        P("ctx", "tp", None),
        P("ctx", "tp"),
        P(None, "tp", None),
        P(None, "tp", None),
        P(None, "tp"),
        P(None, "tp"),
        P(None, "tp"),
        P(None, "tp", None),
    )
    out_specs = P("segment", "ctx", "tp")
    return jax.shard_map(body, mesh=mesh, in_specs=in_specs, out_specs=out_specs, check_vma=False)
```

profile of v0, /device:TPU:255, one launch (start us, length us, event | category | flops | bytes accessed | tf_op | source)
XLA Modules:
  0.0 1027.0 jit_solution(16598531643501486196)
XLA Ops:
  7.4 3.9 fusion.43
  11.4 1.6 copy.52
  13.1 1.6 copy.54
  16.7 5.7 all-reduce.1
  22.5 28.7 %all-reduce.4.cloned.1.call-done = f32[128,1024]{1,0:T(8,128)} async-done(((f32[128,1024]{1,0:T(8,128)}), f32[128,1024]{1,0:T(8,128)}) %all-reduce.4.cloned.1.call-update) | async-done | bytes 524304 | tf_op jit(solution)/shard_map/psum | solution.py:161
  53.1 19.6 %conditional.3 = (f32[128,32]{1,0:T(8,128)}, f32[128,32,64]{0,2,1:T(8,128)S(1)}, f32[32,64,128]{2,1,0:T(8,128)}, f32[32]{0:T(128)}) conditional(s32[]{:T(128)} %convert_element_type.36, () %tuple.55, (s32[]{:T(128)}, f32[128,64]{0,1:T(8,128)S(1)}, f32[128]{0:T(128)S(1)}, f32[1,32]{1,0:T(1,128)S(1)}, f32[1,32]{1,0:T(1,128)S(1)}, ...), branch_computations={%region_10.11_spmd, %region_11.13_spmd} | conditional | flops 860024832 | bytes 13620502 | solution.py:184
  54.8 1.6 exponential_multiply_fusion
  56.4 1.5 copy.45
  61.5 5.2 fusion
  68.4 3.1 fusion.8
  76.8 152.8 %all-reduce = f32[2048]{0:T(1024)S(1)} all-reduce(f32[2048]{0:T(1024)S(1)} %dynamic-update-slice), channel_id=2, replica_groups=mesh['segment'=2,'ctx'=64,'tp'=2] {'ctx'}, use_global_device_ids=true, to_apply=%add | all-reduce | flops 2048 | bytes 16384
  231.2 72.4 %all-gather.8.cloned.1.call-done = bf16[8192,4,128]{2,0,1:T(8,128)(2,1)} async-done(((bf16[128,4,128]{2,0,1:T(8,128)(2,1)}), bf16[8192,4,128]{2,0,1:T(8,128)(2,1)}) %all-gather.8.cloned.1.call-update) | async-done | bytes 8388624 | tf_op jit(solution)/shard_map/all_gather | solution.py:129
  303.6 1.7 conditional.2
  305.3 1.6 fusion.47
  307.9 568.6 %all-gather.10.cloned.1.call-done = f32[2048,64,128]{2,1,0:T(8,128)} async-done(((f32[32,64,128]{2,1,0:T(8,128)}), f32[2048,64,128]{2,1,0:T(8,128)}) %all-gather.10.cloned.1.call-update) | async-done | bytes 67108880 | tf_op jit(solution)/shard_map/all_gather | solution.py:14
  876.6 136.0 %while.30 = (s32[]{:T(128)}, f32[32,64,128]{2,1,0:T(8,128)S(1)}, s32[]{:T(128)}, f32[64,32]{1,0:T(8,128)}, f32[64,32,64,128]{3,2,1,0:T(8,128)}, /*index=5*/s32[]{:T(128)}, s32[]{:T(128)}, s32[]{:T(128)}) while((s32[]{:T(128)}, f32[32,64,128]{2,1,0:T(8,128)S(1)}, s32[]{:T(128)}, f32[64,32]{1,0:T(8,128)}, f32[64,32,64,128]{3,2,1,0:T(8,128)}, ...), condition=%wide.region_14.15_spmd, body=%wide.region_13.14_spmd.sunk | while | flops 524293 | bytes 3146239 | solution.py:22
  877.3 1.4 bitcast_add_fusion.3
  881.7 1.4 bitcast_add_fusion.3
  886.0 1.4 bitcast_add_fusion.3
  890.3 1.4 bitcast_add_fusion.3
  896.7 1.4 bitcast_add_fusion.3
  898.9 1.4 bitcast_add_fusion.3
  901.1 1.4 bitcast_add_fusion.3
  911.8 1.4 bitcast_add_fusion.3
  920.5 1.4 bitcast_add_fusion.3
  922.7 1.4 bitcast_add_fusion.3
  929.2 1.4 bitcast_add_fusion.3
  935.7 1.4 bitcast_add_fusion.3
  940.0 1.4 bitcast_add_fusion.3
  944.3 1.4 bitcast_add_fusion.3
  1015.3 1.6 collective-permute-start
  1016.8 1.5 collective-permute-done
  (178 shorter events, 137.4 us)
Async XLA Ops:
  7.4 9.1 copy-start
  7.4 9.1 copy-start.2
  7.4 45.7 %copy-start.6 = (f32[1,32]{1,0:T(1,128)S(1)}, f32[1,32]{1,0:T(1,128)}, u32[]{:S(2)}) copy-start(f32[1,32]{1,0:T(1,128)} %param.24) | copy-start | bytes 388
  7.4 45.7 %copy-start.7 = (f32[1,32]{1,0:T(1,128)S(1)}, f32[1,32]{1,0:T(1,128)}, u32[]{:S(2)}) copy-start(f32[1,32]{1,0:T(1,128)} %param.25) | copy-start | bytes 388
  7.4 43.8 %all-reduce.4.cloned.1.call-start = ((), (), s32[]{:S(2)}) async-start(), calls=%async_computation.2 | async-start | bytes 1048576 | tf_op jit(solution)/shard_map/psum | solution.py:161
  11.4 219.8 %all-gather.6.cloned.1.call-start = ((), (), s32[]{:S(2)}) async-start(), calls=%async_computation | async-start | bytes 8519680 | tf_op jit(solution)/shard_map/all_gather | solution.py:128
  13.0 290.6 %all-gather.8.cloned.1.call-start = ((), (), s32[]{:S(2)}) async-start(), calls=%async_computation.1 | async-start | bytes 8519680 | tf_op jit(solution)/shard_map/all_gather | solution.py:129
  14.7 861.8 %all-gather.10.cloned.1.call-start = ((), (), s32[]{:S(2)}) async-start(), calls=%async_computation.3 | async-start | bytes 68157440 | tf_op jit(solution)/shard_map/all_gather | solution.py:14
  53.1 4.9 copy-start.5
  59.9 6.8 copy-start.4
  1012.6 2.5 copy-start.3
  1015.3 3.1 collective-permute-start
Sparse Core Ops, SparseCore 0:
  11.5 39.6 all-reduce.3
Sparse Core Ops, SparseCore 1:
  15.4 142.0 all-gather.5
  160.9 142.7 all-gather.7
  307.0 569.5 all-gather.9
where the time goes:
time: 1030 us
  waiting for transfers between devices  671 us (65%)
  blocking collectives  158 us (15%)
  other arithmetic  98.3 us (10%)
  local copies, waits for them, and re-layouts  64.2 us (6%)
  between operations  15.9 us (2%)
  matrix products  14.9 us (1%)
    all_gather x1, waiting for transfers between devices, prefix(): gathered = jax.tree.map(lambda a: lax.all_gather(a, axis), part)  569 us
    unnamed x1, blocking collectives  153 us
    add x63, other arithmetic, merge_states(): later[0][:, None, None] * earlier[1] + later[1]  90.7 us
    all_gather x1, waiting for transfers between devices, body(): value_piece = lax.all_gather(values, 'ctx', axis=0, tiled=True)  72.4 us
    mul x63, local copies, waits for them, and re-layouts, merge_states(): later[0][:, None, None] * earlier[1] + later[1]  43.3 us
    psum x1, waiting for transfers between devices, body(): sum_bc, sum_dt, sum_sq = lax.psum((part_bc, part_dt, part_sq), 'tp')  28.7 us
  transfers between devices with their start and end apart: 5, of which 4 were waited for; matrix products, arithmetic and copies ran while one was open for 3% of the time, Pallas kernels for 0%

commit v1 on v0

--- a/solution.py
+++ b/solution.py
@@ -126,7 +126,9 @@
         jnp.zeros((kv_heads, group_size, row_count, head_width), jnp.float32),
     )
     key_piece = lax.all_gather(keys, "ctx", axis=0, tiled=True)
-    value_piece = lax.all_gather(values, "ctx", axis=0, tiled=True)
+    value_piece = jnp.concatenate(
+        lax.all_to_all(jnp.stack([values] * lax.axis_size("ctx")), "ctx", 0, 0), axis=0
+    )
     key_count = key_piece.shape[0]
     block_size = math.gcd(key_count, 1024)
 

time: 1030 us -> 992 us (0.963)
  waiting for transfers between devices: 671 us -> 404 us
  blocking collectives: 158 us -> 370 us
  starting transfers between devices: 1.72 us -> 14 us
    unnamed x1, blocking collectives: 153 us -> 364 us
    all_gather x1, waiting for transfers between devices: 569 us -> 372 us  [prefix(): gathered = jax.tree.map(lambda a: lax.all_gather(a, axis), part)]
    all_gather x1 -> x0, waiting for transfers between devices: 72.4 us -> none  [body(): value_piece = lax.all_gather(values, 'ctx', axis=0, tiled=True)]
    all_to_all x0 -> x1, starting transfers between devices: none -> 12.4 us  [body(): lax.all_to_all(jnp.stack([values] * lax.axis_size('ctx')), 'ctx', 0, 0)]
  transfers between devices with their start and end apart: 5 -> 5, of which waited for: 4 -> 3; matrix products, arithmetic and copies ran while one was open for 3% -> 4% of each run, Pallas kernels for 0% -> 0%
where the time goes in v1:
time: 992 us; the launch traced here: 986 us
  waiting for transfers between devices  404 us (41%)
  blocking collectives  370 us (37%)
  other arithmetic  98.3 us (10%)
  local copies, waits for them, and re-layouts  67.2 us (7%)
  between operations  15.8 us (2%)
  matrix products  14.9 us (2%)
  starting transfers between devices  14 us (1%)
    all_gather x1, waiting for transfers between devices, prefix(): gathered = jax.tree.map(lambda a: lax.all_gather(a, axis), part)  372 us
    unnamed x1, blocking collectives  364 us
    add x63, other arithmetic, merge_states(): later[0][:, None, None] * earlier[1] + later[1]  90.7 us
    mul x63, local copies, waits for them, and re-layouts, merge_states(): later[0][:, None, None] * earlier[1] + later[1]  43.4 us
    psum x1, waiting for transfers between devices, body(): sum_bc, sum_dt, sum_sq = lax.psum((part_bc, part_dt, part_sq), 'tp')  30.4 us
  transfers between devices with their start and end apart: 5, of which 3 were waited for; matrix products, arithmetic and copies ran while one was open for 4% of the time, Pallas kernels for 0%

profile of v1, /device:TPU:255, one launch (start us, length us, event | category | flops | bytes accessed | tf_op | source)
XLA Modules:
  0.0 986.4 jit_solution(7200397149791931803)
XLA Ops:
  7.4 3.9 fusion.43
  11.4 1.6 copy.53
  15.1 5.7 all-reduce.1
  20.8 30.4 %all-reduce.4.cloned.1.call-done = f32[128,1024]{1,0:T(8,128)} async-done(((f32[128,1024]{1,0:T(8,128)}), f32[128,1024]{1,0:T(8,128)}) %all-reduce.4.cloned.1.call-update) | async-done | bytes 524304 | tf_op jit(solution)/shard_map/psum | solution.py:163
  53.1 19.6 %conditional.3 = (f32[128,32]{1,0:T(8,128)}, f32[128,32,64]{0,2,1:T(8,128)S(1)}, f32[32,64,128]{2,1,0:T(8,128)}, f32[32]{0:T(128)}) conditional(s32[]{:T(128)} %convert_element_type.36, () %tuple.55, (s32[]{:T(128)}, f32[128,64]{0,1:T(8,128)S(1)}, f32[128]{0:T(128)S(1)}, f32[1,32]{1,0:T(1,128)S(1)}, f32[1,32]{1,0:T(1,128)S(1)}, ...), branch_computations={%region_10.11_spmd, %region_11.13_spmd} | conditional | flops 860024832 | bytes 13620502 | solution.py:186
  54.8 1.6 exponential_multiply_fusion
  56.4 1.5 copy.45
  61.5 5.2 fusion
  68.4 3.0 fusion.8
  73.6 5.3 stack.2
  79.0 12.4 %all-to-all-start = ((bf16[64,128,4,128]{3,1,2,0:T(8,128)(2,1)}), bf16[64,128,4,128]{3,1,2,0:T(8,128)(2,1)}, u32[]{:S(2)}, u32[]{:S(2)}) async-start(bf16[64,128,4,128]{3,1,2,0:T(8,128)(2,1)} %stack.2), calls=%async_computation | async-start | bytes 16777216 | tf_op jit(solution)/shard_map/all_to_all | solution.py:130
  93.7 364.1 %all-reduce = f32[2048]{0:T(1024)S(1)} all-reduce(f32[2048]{0:T(1024)S(1)} %dynamic-update-slice), channel_id=2, replica_groups=mesh['segment'=2,'ctx'=64,'tp'=2] {'ctx'}, use_global_device_ids=true, to_apply=%add | all-reduce | flops 2048 | bytes 16384
  459.5 1.7 conditional.2
  461.2 1.6 fusion.47
  463.8 372.3 %all-gather.7.cloned.1.call-done = f32[2048,64,128]{2,1,0:T(8,128)} async-done(((f32[32,64,128]{2,1,0:T(8,128)}), f32[2048,64,128]{2,1,0:T(8,128)}) %all-gather.7.cloned.1.call-update) | async-done | bytes 67108880 | tf_op jit(solution)/shard_map/all_gather | solution.py:14
  836.2 136.1 %while.30 = (s32[]{:T(128)}, f32[32,64,128]{2,1,0:T(8,128)S(1)}, s32[]{:T(128)}, f32[64,32]{1,0:T(8,128)}, f32[64,32,64,128]{3,2,1,0:T(8,128)}, /*index=5*/s32[]{:T(128)}, s32[]{:T(128)}, s32[]{:T(128)}) while((s32[]{:T(128)}, f32[32,64,128]{2,1,0:T(8,128)S(1)}, s32[]{:T(128)}, f32[64,32]{1,0:T(8,128)}, f32[64,32,64,128]{3,2,1,0:T(8,128)}, ...), condition=%wide.region_14.15_spmd, body=%wide.region_13.14_spmd.sunk | while | flops 524293 | bytes 3146239 | solution.py:22
  845.5 1.4 bitcast_add_fusion.3
  847.7 1.4 bitcast_add_fusion.3
  849.9 1.4 bitcast_add_fusion.3
  858.5 1.4 bitcast_add_fusion.3
  860.7 1.4 bitcast_add_fusion.3
  869.3 1.4 bitcast_add_fusion.3
  871.5 1.4 bitcast_add_fusion.3
  882.3 1.4 bitcast_add_fusion.3
  884.4 1.4 bitcast_add_fusion.3
  893.0 1.4 bitcast_add_fusion.3
  897.4 1.4 bitcast_add_fusion.3
  901.7 1.4 bitcast_add_fusion.3
  908.1 1.4 bitcast_add_fusion.3
  910.3 1.4 bitcast_add_fusion.3
  974.9 1.6 collective-permute-start
  976.4 1.5 collective-permute-done
  (182 shorter events, 136.6 us)
Async XLA Ops:
  7.4 7.4 copy-start
  7.4 7.4 copy-start.2
  7.4 45.7 %copy-start.7 = (f32[1,32]{1,0:T(1,128)S(1)}, f32[1,32]{1,0:T(1,128)}, u32[]{:S(2)}) copy-start(f32[1,32]{1,0:T(1,128)} %param.24) | copy-start | bytes 388
  7.4 45.7 %copy-start.8 = (f32[1,32]{1,0:T(1,128)S(1)}, f32[1,32]{1,0:T(1,128)}, u32[]{:S(2)}) copy-start(f32[1,32]{1,0:T(1,128)} %param.25) | copy-start | bytes 388
  7.4 43.8 %all-reduce.4.cloned.1.call-start = ((), (), s32[]{:S(2)}) async-start(), calls=%async_computation.2 | async-start | bytes 1048576 | tf_op jit(solution)/shard_map/psum | solution.py:163
  11.4 448.1 %all-gather.5.cloned.1.call-start = ((), (), s32[]{:S(2)}) async-start(), calls=%async_computation.1 | async-start | bytes 8519680 | tf_op jit(solution)/shard_map/all_gather | solution.py:128
  13.0 823.0 %all-gather.7.cloned.1.call-start = ((), (), s32[]{:S(2)}) async-start(), calls=%async_computation.3 | async-start | bytes 68157440 | tf_op jit(solution)/shard_map/all_gather | solution.py:14
  53.1 4.9 copy-start.6
  60.0 6.8 copy-start.4
  79.0 12.4 %copy-start.5 = (bf16[128,16,128]{2,1,0:T(8,128)(2,1)S(1)}, bf16[128,16,128]{2,1,0:T(8,128)(2,1)}, u32[]{:S(2)}) copy-start(bf16[128,16,128]{2,1,0:T(8,128)(2,1)} %param.18) | copy-start | bytes 1572868
  79.0 12.5 %copy-start.9 = (u32[256]{0:T(256)S(1)}, u32[256]{0:T(256)}, u32[]{:S(2)}) copy-start(u32[256]{0:T(256)} %constant.160) | copy-start | bytes 3076
  79.0 380.5 %all-to-all-start = ((bf16[64,128,4,128]{3,1,2,0:T(8,128)(2,1)}), bf16[64,128,4,128]{3,1,2,0:T(8,128)(2,1)}, u32[]{:S(2)}, u32[]{:S(2)}) async-start(bf16[64,128,4,128]{3,1,2,0:T(8,128)(2,1)} %stack.2), calls=%async_computation | async-start | bytes 16777216 | tf_op jit(solution)/shard_map/all_to_all | solution.py:130
  972.3 2.5 copy-start.3
  974.9 3.1 collective-permute-start
Sparse Core Ops, SparseCore 0:
  11.5 39.6 all-reduce.3
Sparse Core Ops, SparseCore 1:
  15.4 209.4 all-gather.4
  228.2 607.8 all-gather.6
